TPU v7x, 512 devices: a whole 4x4x16 slice. The times are simulated.
512 devices in a mesh: space: 64 (over z_lo, x, core), ky: 8 (over z_hi, y).
Axes of the slice: x: 4, y: 4, z: 16 (z_hi: 2, z_lo: 8; z = z_hi * 8 + z_lo), core: 2. Of those that a mesh axis runs over, the one named last changes fastest.
Arguments:
- distribution: float32 [64, 128, 256, 128], P('space', 'ky'), may hold values from 0 to 2
- region: int32 [64, 256], P('space'), may hold values from 0 to 5, as said below
- region_doping: float32 [6], replicated, may hold values from -1 to 2
- region_relax: float32 [6], replicated, may hold values from 0.2 to 1
- equilibrium: float32 [128, 128], P('ky'), may hold values from 0.3 to 3
- kx_speed: float32 [128], replicated, may hold values from 0.1 to 1
- upwind_sign: int32 [128], replicated, may hold values from -1 to 1, as said below
Outputs:
- advanced: float32 [64, 128, 256, 128], P('space', 'ky')
Inputs may be any that keep to these rules, and one draw needn't show every extreme that they name: region[x, y] = 2 band(y) + m[x, y], with m[x, y] 0 or 1 and band(y) = 0, 1, 2 on three runs of columns, each run at least 32 columns long. `upwind_sign`: exactly 64 entries are 1 and the others -1.
All inputs are finite; a program needn't handle non-finite values.
Results may differ from a plain program's by a relative error of at most 0.0003.
Values sent between devices are 32-bit elements; how exact they have to be, the bound alone decides.
No kernel may reach another device: no remote copies, remote signals or barrier semaphores. Data moves between devices by JAX's collectives and lax.ppermute only.
A program may use at most 64 MiB of HBM per device.

v0:
```python
import math
import jax
import jax.numpy as jnp
from jax import lax
from jax.sharding import PartitionSpec as P

COUPLING = 0.04
POISSON = 0.1
STEP = 0.4
DRIFT_Y = 0.8


def with_halo(block, sides, width):
    for axis, dim in sides:
        count = lax.axis_size(axis)
        forward = [(i, i + 1) for i in range(count - 1)]
        backward = [(target, source) for source, target in forward]
        low = lax.ppermute(
            lax.slice_in_dim(block, block.shape[dim] - width, None, axis=dim), axis, forward
        )
        high = lax.ppermute(lax.slice_in_dim(block, 0, width, axis=dim), axis, backward)
        block = jnp.concatenate([low, block, high], axis=dim)
    return block


def sine_table(length):
    positions = jnp.arange(1, length + 1, dtype=jnp.int32)
    phase_index = positions[:, None] * positions[None, :] % (2 * length + 2)
    return jnp.sqrt(2.0 / (length + 1.0)) * jnp.sin(
        math.pi * phase_index.astype(jnp.float32) / (length + 1.0)
    )


def eigen_values(length):
    positions = jnp.arange(1, length + 1, dtype=jnp.int32).astype(jnp.float32)
    return 4.0 * jnp.sin(0.5 * math.pi * positions / (length + 1.0)) ** 2


def wigner_tables(modes):
    half_count = modes // 2
    shifts = jnp.arange(1, half_count + 1, dtype=jnp.int32)
    wave_index = jnp.arange(modes, dtype=jnp.int32)
    phase_index = shifts[:, None] * wave_index[None, :] % modes
    angles = 2.0 * math.pi / modes * phase_index.astype(jnp.float32)
    forward = jnp.concatenate([jnp.cos(angles), jnp.sin(angles)], axis=0)
    backward = jnp.concatenate([jnp.sin(angles).T, -jnp.cos(angles).T], axis=1)
    return (forward, backward)


def own_differences(potential, modes, first_col, local_cols):
    half_count = modes // 2
    padded = jnp.pad(potential, ((0, 0), (half_count, half_count)))
    window = lax.dynamic_slice_in_dim(padded, first_col, local_cols + 2 * half_count, 1)
    pieces = []
    for offset in range(1, half_count + 1):
        ahead_vals = window[:, half_count + offset : half_count + offset + local_cols]
        behind = window[:, half_count - offset : half_count - offset + local_cols]
        pieces.append(ahead_vals - behind)
    return COUPLING * jnp.stack(pieces, axis=1)


def lookup(region, values_table):
    classes = jnp.arange(values_table.shape[0], dtype=jnp.int32)
    return jnp.sum(jnp.where(region[..., None] == classes, values_table, 0.0), axis=-1)


def shards(distribution, region, region_doping, region_relax, equilibrium, kx_speed, upwind_sign):
    precise = lax.Precision.HIGHEST
    triple = lax.Precision.HIGH
    row_count, ky_local, col_count, kx_count = distribution.shape
    ky_count = ky_local * lax.axis_size("ky")
    grid_rows = row_count * lax.axis_size("space")
    row_start = lax.axis_index("space") * row_count
    partial_value = jnp.sum(distribution, axis=(1, 3)) / (ky_count * kx_count)
    density = lax.psum(partial_value, "ky")
    doping = lookup(region, region_doping)
    relax_rate = lookup(region, region_relax)
    charge = density - doping
    sine_rows = sine_table(grid_rows)
    sine_cols = sine_table(col_count)
    eigen_cols = eigen_values(col_count)
    every_row = lax.all_gather(charge, "space", axis=0, tiled=True)
    along_x = jnp.dot(sine_rows, every_row, precision=precise)
    spectral = jnp.dot(along_x, sine_cols, precision=precise)
    spectral = spectral / (eigen_values(grid_rows)[:, None] + eigen_cols[None, :])
    back_cols = jnp.dot(spectral, sine_cols, precision=precise)
    own_rows = lax.dynamic_slice_in_dim(sine_rows, row_start, row_count, 0)
    potential = POISSON * jnp.dot(own_rows, back_cols, precision=precise)
    spread = lax.all_to_all(distribution, "ky", split_axis=2, concat_axis=1, tiled=True)
    local_cols = spread.shape[2]
    forward, backward = wigner_tables(ky_count)
    weights = own_differences(potential, ky_count, lax.axis_index("ky") * local_cols, local_cols)
    flattened = spread.reshape(row_count, ky_count, local_cols * kx_count)
    coeffs = jnp.einsum("ab,rbm->ram", forward, flattened, precision=triple)
    coeffs = coeffs.reshape(row_count, ky_count, local_cols, kx_count)
    scaled = coeffs * jnp.concatenate([weights, weights], axis=1)[..., None]
    mixed = jnp.einsum(
        "ab,rbm->ram",
        backward,
        scaled.reshape(row_count, ky_count, local_cols * kx_count),
        precision=triple,
    )
    mixed = mixed.reshape(row_count, ky_count, local_cols, kx_count)
    wigner = lax.all_to_all(mixed, "ky", split_axis=1, concat_axis=2, tiled=True)
    positive_kx = upwind_sign > 0
    padded = with_halo(distribution, (("space", 0),), 1)
    from_left = padded[:-2]
    from_right = padded[2:]
    upstream_x = jnp.where(positive_kx[None, None, None, :], from_left, from_right)
    drift_x = -kx_speed[None, None, None, :] * (distribution - upstream_x)
    ky_global = lax.axis_index("ky") * ky_local + jnp.arange(ky_local, dtype=jnp.int32)
    upward = ky_global >= ky_count // 2
    vertical = DRIFT_Y * (ky_global.astype(jnp.float32) + 0.5 - 0.5 * ky_count) / (0.5 * ky_count)
    zero_col = jnp.zeros_like(distribution[:, :, :1])
    from_low = jnp.concatenate([zero_col, distribution[:, :, :-1]], axis=2)
    from_high = jnp.concatenate([distribution[:, :, 1:], zero_col], axis=2)
    upstream_y = jnp.where(upward[None, :, None, None], from_low, from_high)
    drift_y = -jnp.abs(vertical)[None, :, None, None] * (distribution - upstream_y)
    relaxation = relax_rate[:, None, :, None] * (
        density[:, None, :, None] * equilibrium[None, :, None, :] - distribution
    )
    return distribution + STEP * (drift_x + drift_y + wigner + relaxation)


def solution(mesh):
    return jax.shard_map(
        shards,
        mesh=mesh,
        in_specs=(
            P("space", "ky", None, None),
            P("space", None),
            P(),
            P(),
            P("ky", None),
            P(),
            P(),
        ),
        out_specs=P("space", "ky", None, None),
        check_vma=False,
    )
```

profile of v0, /device:TPU:32, one launch (start us, length us, event | category | flops | bytes accessed | tf_op | source)
XLA Modules:
  0.0 378.6 jit_solution(6376607305004779924)
XLA Ops:
  0.0 4.1 %copy.28 = f32[1,16,256,128]{3,1,0,2:T(8,128)} copy(f32[1,16,256,128]{3,2,1,0:T(8,128)} %param.7) | data formatting | bytes 4194304 | tf_op args[0]
  4.1 17.0 %all-to-all-start = ((f32[1,16,256,128]{3,1,0,2:T(8,128)}), f32[1,16,256,128]{3,1,0,2:T(8,128)}, u32[]{:S(2)}, u32[]{:S(2)}) async-start(f32[1,16,256,128]{3,1,0,2:T(8,128)} %copy.28), calls=%async_computation | async-start | bytes 4194304 | tf_op jit(solution)/shard_map/all_to_all | solution.py:89
  21.1 0.2 reduce_sum.29
  21.3 117.8 %psum.7 = f32[1,256]{1,0:T(1,128)S(1)} all-reduce(f32[1,256]{1,0:T(1,128)S(1)} %bitcast.205), channel_id=1, replica_groups=mesh['space'=64,'ky'=8] {'ky'}, use_global_device_ids=true, to_apply=%region_1.0 | all-reduce | flops 256 | bytes 2048 | tf_op jit(solution)/shard_map/psum | solution.py:75
  139.2 0.1 fusion.65
  139.3 105.4 %all-gather = f32[64,1,256]{2,1,0:T(1,128)S(1)} all-gather(f32[1,1,256]{2,1,0:T(1,128)S(1)} %subtract_bitcast_fusion), channel_id=1, replica_groups=mesh['space'=64,'ky'=8] {'space'}, dimensions={0}, use_global_device_ids=true | all-gather | bytes 66560 | tf_op jit(solution)/shard_map/all_gather | solution.py:82
  244.7 0.2 fusion.53
  245.0 0.4 fusion.39
  245.3 1.3 convolution_divide_fusion
  246.7 1.3 fusion.14
  248.0 0.1 fusion.67
  248.2 0.1 fusion.180
  248.3 0.1 copy.84
  248.4 0.1 fusion.174
  248.5 0.1 copy.81
  248.6 0.1 fusion.184
  248.7 0.1 copy.86
  248.8 0.1 fusion.194
  248.9 0.1 copy.91
  249.0 0.1 fusion.196
  249.1 0.1 copy.92
  249.2 0.1 fusion.172
  249.4 0.1 copy.80
  249.4 0.1 fusion.178
  249.6 0.1 copy.83
  249.7 0.1 fusion.186
  249.8 0.1 copy.87
  249.9 0.1 fusion.182
  250.0 0.1 copy.85
  250.1 0.1 fusion.170
  250.2 0.1 copy.79
  250.3 0.1 fusion.192
  250.4 0.1 copy.90
  250.5 0.1 fusion.176
  250.6 0.1 copy.82
  250.7 0.1 fusion.188
  250.8 0.1 copy.88
  250.9 0.1 fusion.168
  251.0 0.1 copy.78
  251.1 0.1 fusion.190
  251.3 0.1 fusion.70
  252.4 0.1 copy.34
  253.0 0.1 copy.57
  254.1 0.1 copy.59
  254.7 0.1 copy.64
  255.7 0.3 stack.259
  256.2 0.1 copy.94
  256.3 1.9 mul.263
  258.2 2.7 mul.264
  260.9 0.2 fusion.62
  261.1 0.3 fusion.54
  261.5 2.4 copy.29
  263.8 2.2 fusion.1
  266.0 3.2 fusion.35
  269.2 3.1 copy.95
  272.3 7.1 %all-to-all-start.1 = ((f32[1,128,32,128]{3,2,0,1:T(8,128)}), f32[1,128,32,128]{3,2,0,1:T(8,128)}, u32[]{:S(2)}, u32[]{:S(2)}) async-start(f32[1,128,32,128]{3,2,0,1:T(8,128)} %copy.95), calls=%async_computation.1 | async-start | bytes 4194304 | tf_op jit(solution)/shard_map/all_to_all | solution.py:104
  279.4 2.4 collective-permute-start.1
  281.8 1.9 collective-permute-start
  283.9 2.5 fusion.209
  286.3 46.5 %all-to-all-done.1 = f32[1,128,32,128]{3,2,0,1:T(8,128)} async-done(((f32[1,128,32,128]{3,2,0,1:T(8,128)}), f32[1,128,32,128]{3,2,0,1:T(8,128)}, u32[]{:S(2)}, u32[]{:S(2)}) %all-to-all-start.1) | async-done | bytes 2097184 | tf_op jit(solution)/shard_map/all_to_all | solution.py:104
  332.9 2.0 copy.96
  334.8 29.5 %collective-permute-done.1 = f32[1,16,256,128]{3,2,1,0:T(8,128)} collective-permute-done((f32[1,16,256,128]{3,2,1,0:T(8,128)S(1)}, f32[1,16,256,128]{3,2,1,0:T(8,128)}, u32[]{:S(2)}, u32[]{:S(2)}) %collective-permute-start.1) | collective-permute-done | bytes 2097184 | tf_op jit(solution)/shard_map/ppermute | solution.py:21
  364.3 8.7 %collective-permute-done = f32[1,16,256,128]{3,2,1,0:T(8,128)} collective-permute-done((f32[1,16,256,128]{3,2,1,0:T(8,128)S(1)}, f32[1,16,256,128]{3,2,1,0:T(8,128)}, u32[]{:S(2)}, u32[]{:S(2)}) %collective-permute-start) | collective-permute-done | bytes 2097184 | tf_op jit(solution)/shard_map/ppermute | solution.py:18
  373.1 5.5 %fusion.6 = f32[1,16,256,128]{3,2,1,0:T(8,128)} fusion(f32[1,16,256,128]{3,2,1,0:T(8,128)S(1)} %copy-done, f32[1,16,8,32,128]{4,3,2,1,0:T(8,128)S(1)} %copy.96, f32[1,16,255,128]{3,2,1,0:T(8,128)S(1)} %copy-done.3, f32[1,16,255,128]{3,2,1,0:T(8,128)S(1)} %copy-done.2, f32[1,16,256,128]{3,2,1,0:T(8,128)} %collective-permute-done, ...), kind=kLoop, calls=%fused_computation.8 | loop fusion | flops 7340032 | bytes 14674640 | tf_op jit(solution)/shard_map/add | solution.py:122
  (80 shorter events, 4.3 us)
Async XLA Ops:
  4.1 17.0 %copy-start = (f32[1,16,256,128]{3,2,1,0:T(8,128)S(1)}, f32[1,16,256,128]{3,2,1,0:T(8,128)}, u32[]{:S(2)}) copy-start(f32[1,16,256,128]{3,2,1,0:T(8,128)} %param.7) | copy-start | bytes 6291460
  4.1 257.3 %all-to-all-start = ((f32[1,16,256,128]{3,1,0,2:T(8,128)}), f32[1,16,256,128]{3,1,0,2:T(8,128)}, u32[]{:S(2)}, u32[]{:S(2)}) async-start(f32[1,16,256,128]{3,1,0,2:T(8,128)} %copy.28), calls=%async_computation | async-start | bytes 4194304 | tf_op jit(solution)/shard_map/all_to_all | solution.py:89
  21.1 118.1 %copy-start.5 = (s32[1,256]{1,0:T(1,128)S(1)}, s32[1,256]{1,0:T(1,128)}, u32[]{:S(2)}) copy-start(s32[1,256]{1,0:T(1,128)} %param.8) | copy-start | bytes 3076
  21.1 118.1 %copy-start.6 = (f32[6]{0:T(128)S(1)}, f32[6]{0:T(128)}, u32[]{:S(2)}) copy-start(f32[6]{0:T(128)} %param.10) | copy-start | bytes 76
  21.1 118.0 %copy-start.7 = (f32[6]{0:T(128)S(1)}, f32[6]{0:T(128)}, u32[]{:S(2)}) copy-start(f32[6]{0:T(128)} %param.9) | copy-start | bytes 76
  261.4 2.4 copy-start.1
  272.3 11.4 %copy-start.8 = (f32[128]{0:T(128)S(1)}, f32[128]{0:T(128)}, u32[]{:S(2)}) copy-start(f32[128]{0:T(128)} %param.12) | copy-start | bytes 1540
  272.3 11.5 %copy-start.9 = (s32[128]{0:T(128)S(1)}, s32[128]{0:T(128)}, u32[]{:S(2)}) copy-start(s32[128]{0:T(128)} %param.13) | copy-start | bytes 1540
  272.3 60.5 %all-to-all-start.1 = ((f32[1,128,32,128]{3,2,0,1:T(8,128)}), f32[1,128,32,128]{3,2,0,1:T(8,128)}, u32[]{:S(2)}, u32[]{:S(2)}) async-start(f32[1,128,32,128]{3,2,0,1:T(8,128)} %copy.95), calls=%async_computation.1 | async-start | bytes 4194304 | tf_op jit(solution)/shard_map/all_to_all | solution.py:104
  279.4 84.9 %collective-permute-start.1 = (f32[1,16,256,128]{3,2,1,0:T(8,128)S(1)}, f32[1,16,256,128]{3,2,1,0:T(8,128)}, u32[]{:S(2)}, u32[]{:S(2)}) collective-permute-start(f32[1,16,256,128]{3,2,1,0:T(8,128)S(1)} %copy-done), channel_id=1, source_target_pairs={{8,0},{16,8},{24,16},{32,24},{40,32},{48,40},{56,48},{64,56},{72,6... | collective-permute-start | bytes 6291464 | tf_op jit(solution)/shard_map/ppermute | solution.py:21
  281.8 91.2 %collective-permute-start = (f32[1,16,256,128]{3,2,1,0:T(8,128)S(1)}, f32[1,16,256,128]{3,2,1,0:T(8,128)}, u32[]{:S(2)}, u32[]{:S(2)}) collective-permute-start(f32[1,16,256,128]{3,2,1,0:T(8,128)S(1)} %copy-done), channel_id=1, source_target_pairs={{0,8},{8,16},{16,24},{24,32},{32,40},{40,48},{48,56},{56,64},{64,7... | collective-permute-start | bytes 6291464 | tf_op jit(solution)/shard_map/ppermute | solution.py:18
  283.8 89.2 %copy-start.4 = (f32[16,128]{1,0:T(8,128)S(1)}, f32[16,128]{1,0:T(8,128)}, u32[]{:S(2)}) copy-start(f32[16,128]{1,0:T(8,128)} %param.11) | copy-start | bytes 24580
  332.9 40.2 %copy-start.2 = (f32[1,16,255,128]{3,2,1,0:T(8,128)S(1)}, f32[1,16,255,128]{3,2,1,0:T(8,128)}, u32[]{:S(2)}) copy-start(f32[1,16,255,128]{3,2,1,0:T(8,128)} %get-tuple-element.7) | copy-start | bytes 6266884
  332.9 40.2 %copy-start.3 = (f32[1,16,255,128]{3,2,1,0:T(8,128)S(1)}, f32[1,16,255,128]{3,2,1,0:T(8,128)}, u32[]{:S(2)}) copy-start(f32[1,16,255,128]{3,2,1,0:T(8,128)} %get-tuple-element.8) | copy-start | bytes 6266884
where the time goes:
time: 379 us
  blocking collectives  223 us (59%)
  waiting for transfers between devices  84.8 us (22%)
  starting transfers between devices  28.4 us (7%)
  local copies, waits for them, and re-layouts  24.8 us (7%)
  other arithmetic  8.64 us (2%)
  matrix products  8.58 us (2%)
    psum x1, blocking collectives, shards(): density = lax.psum(partial_value, 'ky')  118 us
    all_gather x1, blocking collectives, shards(): every_row = lax.all_gather(charge, 'space', axis=0, tiled=True)  105 us
    all_to_all x1, waiting for transfers between devices, shards(): lax.all_to_all(mixed, 'ky', split_axis=1, concat_axis=2, tiled=True)  46.5 us
    ppermute x1, waiting for transfers between devices, with_halo(): lax.ppermute(lax.slice_in_dim(block, 0, width, axis=dim), axis, backward)  29.5 us
    all_to_all x1, starting transfers between devices, shards(): lax.all_to_all(distribution, 'ky', split_axis=2, concat_axis=1, tiled=True)  17 us
    ppermute x1, waiting for transfers between devices, with_halo(): lax.ppermute(lax.slice_in_dim(block, block.shape[dim] - width, None, axis...  8.73 us
  transfers between devices with their start and end apart: 4, of which 3 were waited for; matrix products, arithmetic and copies ran while one was open for 6% of the time, Pallas kernels for 0%

commit v1 on v0

--- a/solution.py
+++ b/solution.py
@@ -101,7 +101,9 @@
         precision=triple,
     )
     mixed = mixed.reshape(row_count, ky_count, local_cols, kx_count)
-    wigner = lax.all_to_all(mixed, "ky", split_axis=1, concat_axis=2, tiled=True)
+    wigner = jnp.concatenate(
+        lax.all_to_all(jnp.stack(jnp.split(mixed, lax.axis_size("ky"), axis=1)), "ky", 0, 0), axis=2
+    )
     positive_kx = upwind_sign > 0
     padded = with_halo(distribution, (("space", 0),), 1)
     from_left = padded[:-2]

time: 379 us -> 409 us (1.079)
  local copies, waits for them, and re-layouts: 24.8 us -> 56.2 us
    ppermute x1, waiting for transfers between devices: 8.73 us -> 39.6 us  [with_halo(): lax.ppermute(lax.slice_in_dim(block, block.shape[dim] - width, None, axis...]
    ppermute x1, waiting for transfers between devices: 29.5 us -> 0.01 us  [with_halo(): lax.ppermute(lax.slice_in_dim(block, 0, width, axis=dim), axis, backward)]
    unnamed x21 -> x36, local copies, waits for them, and re-layouts: 4.19 us -> 30.1 us
    split x0 -> x1, local copies, waits for them, and re-layouts: none -> 7.87 us  [shards(): jnp.split(mixed, lax.axis_size('ky'), axis=1)]
    all_to_all x1, waiting for transfers between devices: 46.5 us -> 41.6 us  [shards(): lax.all_to_all(jnp.stack(jnp.split(mixed, lax.axis_size('ky'), axis=1)),...]
  transfers between devices with their start and end apart: 4 -> 4, of which waited for: 3 -> 2; matrix products, arithmetic and copies ran while one was open for 6% -> 5% of each run, Pallas kernels for 0% -> 0%
where the time goes in v1:
time: 409 us
  blocking collectives  223 us (55%)
  waiting for transfers between devices  81.2 us (20%)
  local copies, waits for them, and re-layouts  56.2 us (14%)
  starting transfers between devices  31.9 us (8%)
  other arithmetic  8.64 us (2%)
  matrix products  7.22 us (2%)
    psum x1, blocking collectives, shards(): density = lax.psum(partial_value, 'ky')  118 us
    all_gather x1, blocking collectives, shards(): every_row = lax.all_gather(charge, 'space', axis=0, tiled=True)  105 us
    all_to_all x1, waiting for transfers between devices, shards(): lax.all_to_all(jnp.stack(jnp.split(mixed, lax.axis_size('ky'), axis=1)),...  41.6 us
    ppermute x1, waiting for transfers between devices, with_halo(): lax.ppermute(lax.slice_in_dim(block, block.shape[dim] - width, None, axis...  39.6 us
    unnamed x36, local copies, waits for them, and re-layouts  30.1 us
    all_to_all x1, starting transfers between devices, shards(): lax.all_to_all(distribution, 'ky', split_axis=2, concat_axis=1, tiled=True)  17 us
  transfers between devices with their start and end apart: 4, of which 2 were waited for; matrix products, arithmetic and copies ran while one was open for 5% of the time, Pallas kernels for 0%

profile of v1, /device:TPU:32, one launch (start us, length us, event | category | flops | bytes accessed | tf_op | source)
XLA Modules:
  0.0 408.7 jit_solution(17277419159128647297)
XLA Ops:
  0.0 4.2 %copy.52 = f32[1,16,256,128]{3,1,0,2:T(8,128)} copy(f32[1,16,256,128]{3,2,1,0:T(8,128)} %param.7) | data formatting | bytes 4194304 | tf_op args[0]
  4.2 17.0 %all-to-all-start = ((f32[1,16,256,128]{3,1,0,2:T(8,128)}), f32[1,16,256,128]{3,1,0,2:T(8,128)}, u32[]{:S(2)}, u32[]{:S(2)}) async-start(f32[1,16,256,128]{3,1,0,2:T(8,128)} %copy.52), calls=%async_computation | async-start | bytes 4194304 | tf_op jit(solution)/shard_map/all_to_all | solution.py:89
  21.2 0.2 reduce_sum.29
  21.4 117.8 %psum.7 = f32[1,256]{1,0:T(1,128)S(1)} all-reduce(f32[1,256]{1,0:T(1,128)S(1)} %bitcast.220), channel_id=1, replica_groups=mesh['space'=64,'ky'=8] {'ky'}, use_global_device_ids=true, to_apply=%region_1.0 | all-reduce | flops 256 | bytes 2048 | tf_op jit(solution)/shard_map/psum | solution.py:75
  139.2 0.1 fusion.65
  139.3 105.4 %all-gather = f32[64,1,256]{2,1,0:T(1,128)S(1)} all-gather(f32[1,1,256]{2,1,0:T(1,128)S(1)} %subtract_bitcast_fusion), channel_id=1, replica_groups=mesh['space'=64,'ky'=8] {'space'}, dimensions={0}, use_global_device_ids=true | all-gather | bytes 66560 | tf_op jit(solution)/shard_map/all_gather | solution.py:82
  244.7 0.2 fusion.53
  245.0 0.4 fusion.39
  245.4 1.3 convolution_divide_fusion
  246.7 1.3 fusion.14
  248.1 0.1 fusion.67
  248.2 0.1 fusion.186
  248.4 0.1 fusion.194
  248.6 0.1 fusion.168
  248.7 0.1 copy.102
  248.8 0.1 fusion.170
  249.0 0.1 fusion.172
  249.2 0.1 fusion.174
  249.4 0.1 copy.105
  249.5 0.1 fusion.176
  249.7 0.1 fusion.178
  249.9 0.1 fusion.180
  250.1 0.1 fusion.182
  250.3 0.1 fusion.184
  250.6 0.1 fusion.188
  250.8 0.1 fusion.190
  251.0 0.1 fusion.192
  251.3 0.1 fusion.196
  251.4 0.1 copy.116
  255.3 0.1 fusion.70
  255.7 0.3 stack.286
  256.2 0.1 copy.118
  256.3 1.9 mul.263
  258.2 2.7 mul.264
  260.9 0.2 fusion.62
  261.2 0.3 fusion.54
  261.5 2.4 copy.53
  263.8 2.2 fusion.1
  266.0 1.8 fusion.35
  267.9 7.9 %fusion.210 = (f32[1,16,32,128]{1,3,2,0:T(8,128)}, f32[1,16,32,128]{1,3,2,0:T(8,128)}, f32[1,16,32,128]{1,3,2,0:T(8,128)}, f32[1,16,32,128]{1,3,2,0:T(8,128)}, f...) fusion(f32[1,128,32,128]{1,3,2,0:T(8,128)S(1)} %bitcast.199), kind=kLoop, calls=%fused_computation.371 | loop fusion | bytes 4194304 | tf_op jit(solution)/shard_map/split | solution.py:105
  275.7 2.2 copy.129
  277.9 0.7 bitcast_dynamic-update-slice_fusion.7
  278.7 2.9 copy.130
  281.6 2.9 copy.131
  284.5 2.2 copy.132
  286.7 2.2 copy.133
  288.9 2.2 copy.134
  291.1 2.2 copy.135
  293.3 2.2 copy.136
  295.5 1.7 bitcast_dynamic-update-slice_fusion.6
  297.2 1.7 bitcast_dynamic-update-slice_fusion.5
  298.9 0.7 bitcast_dynamic-update-slice_fusion.4
  299.6 0.7 bitcast_dynamic-update-slice_fusion.3
  300.3 0.7 bitcast_dynamic-update-slice_fusion.2
  301.0 0.7 bitcast_dynamic-update-slice_fusion.1
  301.7 0.7 bitcast_dynamic-update-slice_fusion
  302.4 7.1 %all-to-all-start.1 = ((f32[8,1,16,32,128]{4,3,2,1,0:T(8,128)}), f32[8,1,16,32,128]{4,3,2,1,0:T(8,128)}, u32[]{:S(2)}, u32[]{:S(2)}) async-start(f32[8,1,16,32,128]{4,3,2,1,0:T(8,128)} %bitcast_dynamic-update-slice_fusion), calls=%async_computation.1 | async-start | bytes 4194304 | tf_op jit(solution)/shard_map/all_to_all | solution.py:105
  309.5 1.9 collective-permute-start
  311.5 5.9 %collective-permute-start.1 = (f32[1,16,256,128]{3,2,1,0:T(8,128)S(1)}, f32[1,16,256,128]{3,2,1,0:T(8,128)}, u32[]{:S(2)}, u32[]{:S(2)}) collective-permute-start(f32[1,16,256,128]{3,2,1,0:T(8,128)S(1)} %copy-done), channel_id=1, source_target_pairs={{8,0},{16,8},{24,16},{32,24},{40,32},{48,40},{56,48},{64,56},{72,6... | collective-permute-start | bytes 6291464 | tf_op jit(solution)/shard_map/ppermute | solution.py:21
  317.5 2.5 fusion.209
  320.0 41.6 %all-to-all-done.1 = f32[8,1,16,32,128]{4,3,2,1,0:T(8,128)} async-done(((f32[8,1,16,32,128]{4,3,2,1,0:T(8,128)}), f32[8,1,16,32,128]{4,3,2,1,0:T(8,128)}, u32[]{:S(2)}, u32[]{:S(2)}) %all-to-all-start.1) | async-done | bytes 2097184 | tf_op jit(solution)/shard_map/all_to_all | solution.py:105
  361.6 2.0 copy.127
  363.6 39.6 %collective-permute-done = f32[1,16,256,128]{3,2,1,0:T(8,128)} collective-permute-done((f32[1,16,256,128]{3,2,1,0:T(8,128)S(1)}, f32[1,16,256,128]{3,2,1,0:T(8,128)}, u32[]{:S(2)}, u32[]{:S(2)}) %collective-permute-start) | collective-permute-done | bytes 2097184 | tf_op jit(solution)/shard_map/ppermute | solution.py:18
  403.2 5.5 %fusion.6 = f32[1,16,256,128]{3,2,1,0:T(8,128)} fusion(f32[1,16,256,128]{3,2,1,0:T(8,128)S(1)} %copy-done, f32[8,1,16,32,128]{4,3,0,2,1:T(8,128)S(1)} %copy.127, f32[1,16,255,128]{3,2,1,0:T(8,128)S(1)} %copy-done.3, f32[1,16,255,128]{3,2,1,0:T(8,128)S(1)} %copy-done.2, f32[1,16,256,128]{3,2,1,0:T(8,128)} %collective-permute-done, ...), kind=kLoop, calls=%fused_computation.8 | loop fusion | flops 7340032 | bytes 14674640 | tf_op jit(solution)/shard_map/add | solution.py:124
  (96 shorter events, 5.6 us)
Async XLA Ops:
  4.2 17.0 %copy-start = (f32[1,16,256,128]{3,2,1,0:T(8,128)S(1)}, f32[1,16,256,128]{3,2,1,0:T(8,128)}, u32[]{:S(2)}) copy-start(f32[1,16,256,128]{3,2,1,0:T(8,128)} %param.7) | copy-start | bytes 6291460
  4.2 257.3 %all-to-all-start = ((f32[1,16,256,128]{3,1,0,2:T(8,128)}), f32[1,16,256,128]{3,1,0,2:T(8,128)}, u32[]{:S(2)}, u32[]{:S(2)}) async-start(f32[1,16,256,128]{3,1,0,2:T(8,128)} %copy.52), calls=%async_computation | async-start | bytes 4194304 | tf_op jit(solution)/shard_map/all_to_all | solution.py:89
  21.1 118.1 %copy-start.5 = (s32[1,256]{1,0:T(1,128)S(1)}, s32[1,256]{1,0:T(1,128)}, u32[]{:S(2)}) copy-start(s32[1,256]{1,0:T(1,128)} %param.8) | copy-start | bytes 3076
  21.1 118.1 %copy-start.6 = (f32[6]{0:T(128)S(1)}, f32[6]{0:T(128)}, u32[]{:S(2)}) copy-start(f32[6]{0:T(128)} %param.10) | copy-start | bytes 76
  21.1 118.0 %copy-start.7 = (f32[6]{0:T(128)S(1)}, f32[6]{0:T(128)}, u32[]{:S(2)}) copy-start(f32[6]{0:T(128)} %param.9) | copy-start | bytes 76
  261.4 2.4 copy-start.1
  302.4 15.0 %copy-start.8 = (f32[128]{0:T(128)S(1)}, f32[128]{0:T(128)}, u32[]{:S(2)}) copy-start(f32[128]{0:T(128)} %param.12) | copy-start | bytes 1540
  302.4 15.0 %copy-start.9 = (s32[128]{0:T(128)S(1)}, s32[128]{0:T(128)}, u32[]{:S(2)}) copy-start(s32[128]{0:T(128)} %param.13) | copy-start | bytes 1540
  302.4 59.1 %all-to-all-start.1 = ((f32[8,1,16,32,128]{4,3,2,1,0:T(8,128)}), f32[8,1,16,32,128]{4,3,2,1,0:T(8,128)}, u32[]{:S(2)}, u32[]{:S(2)}) async-start(f32[8,1,16,32,128]{4,3,2,1,0:T(8,128)} %bitcast_dynamic-update-slice_fusion), calls=%async_computation.1 | async-start | bytes 4194304 | tf_op jit(solution)/shard_map/all_to_all | solution.py:105
  309.5 93.6 %collective-permute-start = (f32[1,16,256,128]{3,2,1,0:T(8,128)S(1)}, f32[1,16,256,128]{3,2,1,0:T(8,128)}, u32[]{:S(2)}, u32[]{:S(2)}) collective-permute-start(f32[1,16,256,128]{3,2,1,0:T(8,128)S(1)} %copy-done), channel_id=1, source_target_pairs={{0,8},{8,16},{16,24},{24,32},{32,40},{40,48},{48,56},{56,64},{64,7... | collective-permute-start | bytes 6291464 | tf_op jit(solution)/shard_map/ppermute | solution.py:18
  311.5 91.7 %collective-permute-start.1 = (f32[1,16,256,128]{3,2,1,0:T(8,128)S(1)}, f32[1,16,256,128]{3,2,1,0:T(8,128)}, u32[]{:S(2)}, u32[]{:S(2)}) collective-permute-start(f32[1,16,256,128]{3,2,1,0:T(8,128)S(1)} %copy-done), channel_id=1, source_target_pairs={{8,0},{16,8},{24,16},{32,24},{40,32},{48,40},{56,48},{64,56},{72,6... | collective-permute-start | bytes 6291464 | tf_op jit(solution)/shard_map/ppermute | solution.py:21
  317.5 85.7 %copy-start.4 = (f32[16,128]{1,0:T(8,128)S(1)}, f32[16,128]{1,0:T(8,128)}, u32[]{:S(2)}) copy-start(f32[16,128]{1,0:T(8,128)} %param.11) | copy-start | bytes 24580
  361.6 41.6 %copy-start.2 = (f32[1,16,255,128]{3,2,1,0:T(8,128)S(1)}, f32[1,16,255,128]{3,2,1,0:T(8,128)}, u32[]{:S(2)}) copy-start(f32[1,16,255,128]{3,2,1,0:T(8,128)} %get-tuple-element.7) | copy-start | bytes 6266884
  361.6 41.6 %copy-start.3 = (f32[1,16,255,128]{3,2,1,0:T(8,128)S(1)}, f32[1,16,255,128]{3,2,1,0:T(8,128)}, u32[]{:S(2)}) copy-start(f32[1,16,255,128]{3,2,1,0:T(8,128)} %get-tuple-element.8) | copy-start | bytes 6266884
